TPU v7x, 128 devices: a whole 4x4x4 slice. The times are simulated.
128 devices in a mesh: ra: 16 (over z, y), dec: 8 (over x, core).
Axes of the slice: x: 4, y: 4, z: 4, core: 2. Of those that a mesh axis runs over, the one named last changes fastest.
Arguments:
- features: bfloat16 [512, 256, 128], P('ra', 'dec'), may hold values from -6 to 6
- conv_weight: bfloat16 [3, 3, 128, 128], replicated, may hold values from -0.1875 to 0.1875
- conv_bias: float32 [128], replicated, may hold values from -3 to 3
- corners: int32 [16, 8, 200, 2], P('ra', 'dec'), may hold values from 0 to 25
- owner_ids: int32 [16, 8, 200, 1], P('ra', 'dec'), may hold values from 0 to 127; in each aligned block of 200 rows (0 to 199, 200 to 399, ..., all dimensions but the last counted through in order) at most 3 rows name the same one
- labels: int32 [16, 8, 200], P('ra', 'dec'), may hold values from 0 to 2
- head_w1: bfloat16 [128, 6272, 512], P(('ra', 'dec')), may hold values from -0.078125 to 0.078125
- head_b1: float32 [128, 512], P(('ra', 'dec')), may hold values from -3 to 3
- head_w2: bfloat16 [128, 512, 3], P(('ra', 'dec')), may hold values from -1 to 1
- head_b2: float32 [128, 3], P(('ra', 'dec')), may hold values from -4 to 4
Outputs:
- grad_features: bfloat16 [512, 256, 128], P('ra', 'dec')
- grad_conv: float32 [3, 3, 128, 128], replicated
- grad_w1: bfloat16 [128, 6272, 512], P(('ra', 'dec'))
Inputs may be any that keep to these rules, and one draw needn't show every extreme that they name: `corners`: every crop lies inside its own tile. `owner_ids`: at most 3 objects of one tile go to one expert, and every expert gets some object.
All inputs are finite; a program needn't handle non-finite values.
Results may differ from a plain program's by a relative error of at most 0.0095.
Values may be sent and summed in bfloat16 or wider, within the bound.
No kernel may reach another device: no remote copies, remote signals or barrier semaphores. Data moves between devices by JAX's collectives and lax.ppermute only.
A program may use at most 128 MiB of HBM per device.

v0:
```python
import jax
import jax.numpy as jnp
from jax import lax
from jax.sharding import PartitionSpec as P

CROP = 7


loss_scale = 8.0


def padded_2(cells, sides, width):
    for axis, dim in sides:
        count = lax.axis_size(axis)
        ends = count - 1
        head = lax.slice_in_dim(cells, 0, width, axis=dim)
        tail = lax.slice_in_dim(cells, cells.shape[dim] - width, cells.shape[dim], axis=dim)
        cells = jnp.concatenate(
            [
                lax.ppermute(tail, axis, [(i, (i + 1) % count) for i in range(ends)]),
                cells,
                lax.ppermute(head, axis, [((i + 1) % count, i) for i in range(ends)]),
            ],
            axis=dim,
        )
    return cells


def silu_slope(value):
    logistic = jax.nn.sigmoid(value)
    return logistic * (1.0 + value * (1.0 - logistic))


def rank_in_owner(owner_list, owners_all):
    onehot = (owner_list[:, None] == jnp.arange(owners_all, dtype=jnp.int32)[None, :]).astype(
        jnp.int32
    )
    running = jnp.cumsum(onehot, axis=0)
    return jnp.sum(running * onehot, axis=1) - 1


def head_pass(crop_rows, target_rows, weight_one, bias_one, weight_two, bias_two):
    hid_pre = jnp.dot(crop_rows, weight_one, preferred_element_type=jnp.float32) + bias_one[None, :]
    hidden = jax.nn.silu(hid_pre).astype(jnp.bfloat16)
    logits = jnp.dot(hidden, weight_two, preferred_element_type=jnp.float32) + bias_two[None, :]
    target = target_rows.astype(jnp.float32)
    live_float = jnp.sum(target, axis=1, keepdims=True)
    dlogit = (loss_scale * (live_float * jax.nn.sigmoid(logits) - target)).astype(jnp.bfloat16)
    hid_grad = lax.dot_general(
        dlogit, weight_two, (((1,), (1,)), ((), ())), preferred_element_type=jnp.float32
    )
    hid_grad = (hid_grad * silu_slope(hid_pre)).astype(jnp.bfloat16)
    grad_one = lax.dot_general(
        crop_rows, hid_grad, (((0,), (0,)), ((), ())), preferred_element_type=jnp.float32
    )
    crop_grad = lax.dot_general(
        hid_grad, weight_one, (((1,), (1,)), ((), ())), preferred_element_type=jnp.float32
    )
    return (grad_one.astype(jnp.bfloat16), crop_grad.astype(jnp.bfloat16))


def local(
    features, conv_weight, conv_bias, corners, owner_ids, labels, head_w1, head_b1, head_w2, head_b2
):
    tile_rows, tile_cols, channels = features.shape
    padded = padded_2(features, (("ra", 0), ("dec", 1)), 1)
    pre_conv = jnp.zeros((tile_rows * tile_cols, channels), jnp.float32)
    for row_off in range(3):
        for col_off in range(3):
            window = padded[row_off : row_off + tile_rows, col_off : col_off + tile_cols].reshape(
                -1, channels
            )
            pre_conv = pre_conv + jnp.dot(
                window, conv_weight[row_off, col_off], preferred_element_type=jnp.float32
            )
    pre_conv = (pre_conv + conv_bias[None, :]).reshape(tile_rows, tile_cols, channels)
    activation = jax.nn.silu(pre_conv).astype(jnp.bfloat16)
    count_ra = lax.axis_size("ra")
    count_dec = lax.axis_size("dec")
    owners_all = count_ra * count_dec
    owner_list = owner_ids.reshape(-1)
    corner_list = corners.reshape(-1, 2)
    object_count = owner_list.shape[0]
    capacity = (object_count + owners_all - 1) // owners_all + 1
    slot_total = owners_all * capacity
    classes = head_w2.shape[2]
    crop_size = CROP * CROP * channels
    slot_rank = rank_in_owner(owner_list, owners_all)
    slot_index = owner_list * capacity + slot_rank
    offsets = jnp.arange(CROP, dtype=jnp.int32)
    row_index = corner_list[:, 0][:, None, None] + offsets[None, :, None]
    col_index = corner_list[:, 1][:, None, None] + offsets[None, None, :]
    crop_rows = activation[row_index, col_index].reshape(object_count, crop_size)
    onehot_label = (
        labels.reshape(-1)[:, None] == jnp.arange(classes, dtype=jnp.int32)[None, :]
    ).astype(jnp.bfloat16)
    slot_object = (
        jnp.full((slot_total,), -1, jnp.int32)
        .at[slot_index]
        .set(jnp.arange(object_count, dtype=jnp.int32))
    )
    slot_live = slot_object >= 0
    slot_safe = jnp.where(slot_live, slot_object, 0)
    send_rows = jnp.where(
        slot_live[:, None], jnp.take(crop_rows, slot_safe, axis=0), jnp.zeros((), jnp.bfloat16)
    )
    send_target = jnp.where(
        slot_live[:, None], jnp.take(onehot_label, slot_safe, axis=0), jnp.zeros((), jnp.bfloat16)
    )
    weight_one = head_w1[0]
    bias_one = head_b1[0]
    weight_two = head_w2[0]
    bias_two = head_b2[0]
    got_rows, got_target = (
        lax.all_to_all(
            send_rows.reshape(owners_all, capacity, crop_size),
            ("ra", "dec"),
            split_axis=0,
            concat_axis=0,
            tiled=True,
        ),
        lax.all_to_all(
            send_target.reshape(owners_all, capacity, classes),
            ("ra", "dec"),
            split_axis=0,
            concat_axis=0,
            tiled=True,
        ),
    )
    grad_one, crop_grad = head_pass(
        got_rows.reshape(-1, crop_size),
        got_target.reshape(-1, classes),
        weight_one,
        bias_one,
        weight_two,
        bias_two,
    )
    returned = lax.all_to_all(
        crop_grad.reshape(owners_all, capacity, crop_size),
        ("ra", "dec"),
        split_axis=0,
        concat_axis=0,
        tiled=True,
    )
    back_rows = jnp.take(returned.reshape(-1, crop_size), slot_index, axis=0)
    values = back_rows.reshape(object_count, CROP, CROP, channels).astype(jnp.float32)
    act_grad = (
        jnp.zeros((tile_rows, tile_cols, channels), jnp.float32)
        .at[row_index, col_index]
        .add(values)
    )
    pre_grad = (act_grad * silu_slope(pre_conv)).astype(jnp.bfloat16)
    grad_padded = padded_2(pre_grad, (("ra", 0), ("dec", 1)), 1)
    pre_flat = pre_grad.reshape(-1, channels)
    tap_list = []
    grad_feat = jnp.zeros((tile_rows * tile_cols, channels), jnp.float32)
    for row_off in range(3):
        for col_off in range(3):
            window = padded[row_off : row_off + tile_rows, col_off : col_off + tile_cols].reshape(
                -1, channels
            )
            tap_list.append(
                lax.dot_general(
                    window, pre_flat, (((0,), (0,)), ((), ())), preferred_element_type=jnp.float32
                )
            )
            shifted = grad_padded[
                2 - row_off : 2 - row_off + tile_rows, 2 - col_off : 2 - col_off + tile_cols
            ].reshape(-1, channels)
            grad_feat = grad_feat + lax.dot_general(
                shifted,
                conv_weight[row_off, col_off],
                (((1,), (1,)), ((), ())),
                preferred_element_type=jnp.float32,
            )
    local_taps = jnp.stack(tap_list).reshape(3, 3, channels, channels)
    grad_conv = lax.psum(local_taps, ("ra", "dec"))
    grad_features = grad_feat.reshape(tile_rows, tile_cols, channels).astype(jnp.bfloat16)
    return (grad_features, grad_conv, grad_one[None])


def solution(mesh):
    in_specs = (
        P("ra", "dec", None),
        P(),
        P(),
        P("ra", "dec", None, None),
        P("ra", "dec", None, None),
        P("ra", "dec", None),
        P(("ra", "dec"), None, None),
        P(("ra", "dec"), None),
        P(("ra", "dec"), None, None),
        P(("ra", "dec"), None),
    )
    out_specs = (P("ra", "dec", None), P(), P(("ra", "dec"), None, None))
    return jax.shard_map(local, mesh=mesh, in_specs=in_specs, out_specs=out_specs, check_vma=False)
```

profile of v0, /device:TPU:1, one launch (start us, length us, event | category | flops | bytes accessed | tf_op | source)
XLA Modules:
  0.0 652.4 jit_solution(923496613759407383)
XLA Ops:
  7.2 0.8 iota_compare_fusion.1
  8.3 0.9 fusion.48
  9.1 0.7 compare_select_fusion.2
  9.8 1.2 scatter_custom_fusion
  11.1 0.8 fusion.49
  11.9 1.4 gather_fusion
  13.4 0.3 gather.22
  13.9 0.2 broadcast_in_dim.101
  14.2 0.7 copy.30
  14.9 11.5 %all-to-all-start = ((bf16[128,3,3]{1,2,0:T(4,128)(2,1)}), bf16[128,3,3]{1,2,0:T(4,128)(2,1)S(1)}, u32[]{:S(2)}, u32[]{:S(2)}) async-start(bf16[128,3,3]{1,2,0:T(4,128)(2,1)} %copy.30), calls=%async_computation | async-start | bytes 262144 | tf_op jit(solution)/shard_map/all_to_all | solution.py:122
  26.4 0.7 fusion.106
  27.2 3.3 collective-permute-start
  30.4 1.3 collective-permute-start.1
  31.7 0.8 fusion.107
  32.8 0.3 broadcast_or_fusion
  33.1 0.4 reshape.291
  33.5 1.1 constant_dynamic-update-slice_fusion.3
  34.7 0.5 collective-permute-done.1
  35.2 4.5 collective-permute-start.2
  39.7 2.1 collective-permute-start.3
  42.3 2.4 collective-permute-done.3
  44.7 0.3 pad_maximum_fusion.4
  46.9 107.8 %gather_fusion.1 = bf16[9800,128]{1,0:T(8,128)(2,1)} fusion(bf16[32,32,128]{2,1,0:T(8,128)(2,1)S(1)} %multiply_convert_fusion.4, s32[9800]{0:T(1024)S(1)} %reshape.291), kind=kCustom, calls=%fused_computation.1 | custom fusion | bytes 5096000 | tf_op jit(solution)/shard_map/gather | solution.py:93
  154.6 4.5 reshape.263
  159.2 5.8 gather_fusion.2
  165.0 11.5 %gather.25 = bf16[128,3,6272]{2,1,0:T(4,128)(2,1)} reshape(bf16[384,6272]{1,0:T(8,128)(2,1)} %gather_fusion.2) | data formatting | bytes 9633792 | tf_op jit(solution)/shard_map/jit(_take)/gather | solution.py:105
  176.4 9.0 %select_select_fusion = bf16[128,3,6272]{2,1,0:T(4,128)(2,1)} fusion(bf16[128,3,6272]{2,1,0:T(4,128)(2,1)} %gather.25, pred[128,3]{1,0:T(8,128)(4,1)S(1)} %broadcast_in_dim.103, pred[128,3]{1,0:T(8,128)(4,1)S(1)} %broadcast_in_dim.101), kind=kLoop, calls=%fused_computation.12 | loop fusion | flops 4816896 | bytes 9634560 | tf_op jit(solution)/shard_map/jit(_where)/select_n | solution.py:104
  185.4 11.1 %all-to-all-start.1 = ((bf16[128,3,6272]{2,1,0:T(4,128)(2,1)}), bf16[128,3,6272]{2,1,0:T(4,128)(2,1)}, u32[]{:S(2)}, u32[]{:S(2)}) async-start(bf16[128,3,6272]{2,1,0:T(4,128)(2,1)} %select_select_fusion), calls=%async_computation.1 | async-start | bytes 12845056 | tf_op jit(solution)/shard_map/all_to_all | solution.py:115
  197.2 76.0 %all-to-all-done.1 = bf16[128,3,6272]{2,1,0:T(4,128)(2,1)} async-done(((bf16[128,3,6272]{2,1,0:T(4,128)(2,1)}), bf16[128,3,6272]{2,1,0:T(4,128)(2,1)}, u32[]{:S(2)}, u32[]{:S(2)}) %all-to-all-start.1) | async-done | bytes 4816928 | tf_op jit(solution)/shard_map/all_to_all | solution.py:115
  273.2 12.4 %reshape.264 = bf16[384,6272]{1,0:T(8,128)(2,1)} reshape(bf16[128,3,6272]{2,1,0:T(4,128)(2,1)} %all-to-all-done.1) | data formatting | bytes 9633792 | tf_op jit(solution)/shard_map/reshape | solution.py:131
  285.6 6.3 fusion.4
  292.0 0.8 fusion.7
  292.7 8.7 %convolution_convert_fusion.1 = bf16[384,6272]{1,0:T(8,128)(2,1)} fusion(bf16[384,512]{1,0:T(8,128)(2,1)S(1)} %fusion.7, bf16[1,6272,512]{2,1,0:T(8,128)(2,1)} %param.16), kind=kOutput, calls=%fused_computation.7 | convolution fusion | flops 2468659200 | bytes 11632640 | tf_op jit(solution)/shard_map/dot_general | solution.py:56
  301.5 11.5 %reshape.265 = bf16[128,3,6272]{2,1,0:T(4,128)(2,1)} reshape(bf16[384,6272]{1,0:T(8,128)(2,1)} %convolution_convert_fusion.1) | data formatting | bytes 9633792 | tf_op jit(solution)/shard_map/reshape | solution.py:139
  313.0 6.5 %all-to-all-start.2 = ((bf16[128,3,6272]{2,1,0:T(4,128)(2,1)}), bf16[128,3,6272]{2,1,0:T(4,128)(2,1)}, u32[]{:S(2)}, u32[]{:S(2)}) async-start(bf16[128,3,6272]{2,1,0:T(4,128)(2,1)} %reshape.265), calls=%async_computation.2 | async-start | bytes 12845056 | tf_op jit(solution)/shard_map/all_to_all | solution.py:138
  319.6 0.2 and_reduce_fusion
  320.1 0.4 copy.26
  320.5 0.4 reshape.321
  321.0 7.8 %fusion = bf16[1,6272,512]{2,1,0:T(8,128)(2,1)} fusion(bf16[384,6272]{1,0:T(8,128)(2,1)} %reshape.264, bf16[384,512]{1,0:T(8,128)(2,1)S(1)} %fusion.7), kind=kOutput, calls=%fused_computation.8 | convolution fusion | flops 2469462016 | bytes 11632640 | tf_op jit(solution)/shard_map/dot_general | solution.py:53
  328.8 67.3 %all-to-all-done.2 = bf16[128,3,6272]{2,1,0:T(4,128)(2,1)} async-done(((bf16[128,3,6272]{2,1,0:T(4,128)(2,1)}), bf16[128,3,6272]{2,1,0:T(4,128)(2,1)}, u32[]{:S(2)}, u32[]{:S(2)}) %all-to-all-start.2) | async-done | bytes 4816928 | tf_op jit(solution)/shard_map/all_to_all | solution.py:138
  396.1 12.4 %reshape.266 = bf16[384,6272]{1,0:T(8,128)(2,1)} reshape(bf16[128,3,6272]{2,1,0:T(4,128)(2,1)} %all-to-all-done.2) | data formatting | bytes 9633792 | tf_op jit(solution)/shard_map/reshape | solution.py:145
  408.6 8.9 %gather_fusion.3 = bf16[200,6272]{1,0:T(8,128)(2,1)} fusion(bf16[384,6272]{1,0:T(8,128)(2,1)} %reshape.266, s32[1024]{0:T(1024)S(1)} %pad_clamp_fusion), kind=kCustom, calls=%fused_computation.3 | custom fusion | bytes 5018400 | tf_op jit(solution)/shard_map/jit(_take)/gather | solution.py:145
  417.5 5.2 gather.27
  422.6 3.0 select_convert_fusion
  425.6 6.7 %reshape.323 = f32[9800,128]{1,0:T(8,128)} reshape(f32[200,7,7,128]{3,2,1,0:T(8,128)} %select_convert_fusion) | data formatting | bytes 10035200 | tf_op jit(solution)/shard_map/convert_element_type | solution.py:146
  432.3 55.8 %scatter_custom_fusion.1 = f32[1024,128]{1,0:T(8,128)S(1)} fusion(s32[9800]{0:T(1024)S(1)} %reshape.321, f32[9800,128]{1,0:T(8,128)} %reshape.323, f32[]{:T(128)} %constant.27.clone.1), kind=kCustom, calls=%fused_computation.90 | custom fusion | flops 1254400 | bytes 524800
  488.4 0.3 fusion.21
  488.6 1.3 collective-permute-start.5
  489.9 4.0 collective-permute-start.4
  493.9 1.2 fusion.14
  495.2 0.3 fusion.20
  495.5 0.3 fusion.19
  495.7 0.3 fusion.18
  496.0 0.3 fusion.17
  496.3 0.3 fusion.16
  496.6 0.3 fusion.13
  496.9 0.3 fusion.15
  497.2 0.8 copy-done.20
  498.1 3.3 collective-permute-start.6
  501.4 3.4 collective-permute-start.7
  505.1 0.6 collective-permute-done.7
  507.8 0.9 fusion.12
  508.7 135.0 %all-reduce.3.cloned.1.call-done = f32[3,3,128,128]{3,2,1,0:T(8,128)} async-done(((f32[3,3,128,128]{3,2,1,0:T(8,128)}), f32[3,3,128,128]{3,2,1,0:T(8,128)}) %all-reduce.3.cloned.1.call-update) | async-done | bytes 589840 | tf_op jit(solution)/shard_map/psum | solution.py:177
  643.7 1.9 copy.52
  (120 shorter events, 6.6 us)
Async XLA Ops:
  7.2 284.8 %copy-start = (bf16[1,512,3]{1,2,0:T(4,128)(2,1)S(1)}, bf16[1,512,3]{1,2,0:T(4,128)(2,1)}, u32[]{:S(2)}) copy-start(bf16[1,512,3]{1,2,0:T(4,128)(2,1)} %param.18) | copy-start | bytes 9220
  7.2 34.7 %copy-start.4 = (bf16[3,3,128,128]{3,2,1,0:T(8,128)(2,1)S(1)}, bf16[3,3,128,128]{3,2,1,0:T(8,128)(2,1)}, u32[]{:S(2)}) copy-start(bf16[3,3,128,128]{3,2,1,0:T(8,128)(2,1)} %param.11) | copy-start | bytes 884740
  14.9 170.5 %all-to-all-start = ((bf16[128,3,3]{1,2,0:T(4,128)(2,1)}), bf16[128,3,3]{1,2,0:T(4,128)(2,1)S(1)}, u32[]{:S(2)}, u32[]{:S(2)}) async-start(bf16[128,3,3]{1,2,0:T(4,128)(2,1)} %copy.30), calls=%async_computation | async-start | bytes 262144 | tf_op jit(solution)/shard_map/all_to_all | solution.py:122
  27.2 6.4 collective-permute-start
  30.4 4.7 collective-permute-start.1
  33.1 12.9 %copy-start.2 = (bf16[32,32,128]{2,1,0:T(8,128)(2,1)S(1)}, bf16[32,32,128]{2,1,0:T(8,128)(2,1)}, u32[]{:S(2)}) copy-start(bf16[32,32,128]{2,1,0:T(8,128)(2,1)} %param.10) | copy-start | bytes 786436
  34.7 7.6 %copy-start.21 = (bf16[33,32,128]{2,1,0:T(8,128)(2,1)}, bf16[33,32,128]{2,1,0:T(8,128)(2,1)S(1)}, u32[]{:S(2)}) copy-start(bf16[33,32,128]{2,1,0:T(8,128)(2,1)S(1)} %get-tuple-element.28) | copy-start | bytes 811012
  35.1 6.7 %copy-start.18 = (bf16[33,32,128]{2,1,0:T(8,128)(2,1)}, bf16[33,32,128]{2,1,0:T(8,128)(2,1)S(1)}, u32[]{:S(2)}) copy-start(bf16[33,32,128]{2,1,0:T(8,128)(2,1)S(1)} %get-tuple-element.35) | copy-start | bytes 811012
  35.2 7.1 %collective-permute-start.2 = (bf16[34,1,128]{2,1,0:T(2,128)(2,1)S(1)}, bf16[34,1,128]{2,1,0:T(2,128)(2,1)S(1)}, u32[]{:S(2)}, u32[]{:S(2)}) collective-permute-start(bf16[34,1,128]{2,1,0:T(2,128)(2,1)S(1)} %get-tuple-element.22), channel_id=1, source_target_pairs={{0,1},{1,2},{2,3},{3,4},{4,5},{5,6},{6,7},{8,9},{9,10},{10,11},{11... | collective-permute-start | bytes 26120 | tf_op jit(solution)/shard_map/ppermute | solution.py:20
  39.7 5.1 collective-permute-start.3
  41.8 4.7 copy-start.24
  45.1 1.2 copy-start.6
  45.1 1.6 copy-start.12
  45.1 1.6 copy-start.14
  45.1 1.6 copy-start.16
  45.1 1.8 copy-start.8
  45.1 1.8 copy-start.10
  185.4 87.7 %all-to-all-start.1 = ((bf16[128,3,6272]{2,1,0:T(4,128)(2,1)}), bf16[128,3,6272]{2,1,0:T(4,128)(2,1)}, u32[]{:S(2)}, u32[]{:S(2)}) async-start(bf16[128,3,6272]{2,1,0:T(4,128)(2,1)} %select_select_fusion), calls=%async_computation.1 | async-start | bytes 12845056 | tf_op jit(solution)/shard_map/all_to_all | solution.py:115
  196.8 88.8 %copy-start.25 = (f32[1,512]{1,0:T(1,128)S(1)}, f32[1,512]{1,0:T(1,128)}, u32[]{:S(2)}) copy-start(f32[1,512]{1,0:T(1,128)} %param.17) | copy-start | bytes 6148
  285.6 6.4 copy-start.26
  313.0 6.9 %copy-start.23 = (s32[2]{0:T(128)S(1)}, s32[2]{0:T(128)}, u32[]{:S(2)}) copy-start(s32[2]{0:T(128)} %constant.87) | copy-start | bytes 28
  313.0 8.0 %copy-start.22 = (s32[1,1,200,1]{2,3,1,0:T(1,128)S(1)}, s32[1,1,200,1]{2,3,1,0:T(1,128)}, u32[]{:S(2)}) copy-start(s32[1,1,200,1]{2,3,1,0:T(1,128)} %param.14) | copy-start | bytes 2404
  313.0 83.2 %all-to-all-start.2 = ((bf16[128,3,6272]{2,1,0:T(4,128)(2,1)}), bf16[128,3,6272]{2,1,0:T(4,128)(2,1)}, u32[]{:S(2)}, u32[]{:S(2)}) async-start(bf16[128,3,6272]{2,1,0:T(4,128)(2,1)} %reshape.265), calls=%async_computation.2 | async-start | bytes 12845056 | tf_op jit(solution)/shard_map/all_to_all | solution.py:138
  319.5 324.1 %all-reduce.3.cloned.1.call-start = ((), (), s32[]{:S(2)}) async-start(), calls=%async_computation.3 | async-start | bytes 1179648 | tf_op jit(solution)/shard_map/psum | solution.py:177
  425.6 62.7 %copy-start.15 = (bf16[32,32,128]{2,1,0:T(8,128)(2,1)S(1)}, bf16[32,32,128]{2,1,0:T(8,128)(2,1)}, u32[]{:S(2)}) copy-start(bf16[32,32,128]{2,1,0:T(8,128)(2,1)} %copy-done.14) | copy-start | bytes 786436
  425.6 69.5 %copy-start.13 = (bf16[32,32,128]{2,1,0:T(8,128)(2,1)S(1)}, bf16[32,32,128]{2,1,0:T(8,128)(2,1)}, u32[]{:S(2)}) copy-start(bf16[32,32,128]{2,1,0:T(8,128)(2,1)} %copy-done.12) | copy-start | bytes 786436
  425.6 69.8 %copy-start.11 = (bf16[32,32,128]{2,1,0:T(8,128)(2,1)S(1)}, bf16[32,32,128]{2,1,0:T(8,128)(2,1)}, u32[]{:S(2)}) copy-start(bf16[32,32,128]{2,1,0:T(8,128)(2,1)} %copy-done.10) | copy-start | bytes 786436
  425.6 70.1 %copy-start.3 = (bf16[32,32,128]{2,1,0:T(8,128)(2,1)S(1)}, bf16[32,32,128]{2,1,0:T(8,128)(2,1)}, u32[]{:S(2)}) copy-start(bf16[32,32,128]{2,1,0:T(8,128)(2,1)} %param.10) | copy-start | bytes 786436
  432.3 63.7 %copy-start.9 = (bf16[32,32,128]{2,1,0:T(8,128)(2,1)S(1)}, bf16[32,32,128]{2,1,0:T(8,128)(2,1)}, u32[]{:S(2)}) copy-start(bf16[32,32,128]{2,1,0:T(8,128)(2,1)} %copy-done.8) | copy-start | bytes 786436
  432.3 64.6 %copy-start.7 = (bf16[32,32,128]{2,1,0:T(8,128)(2,1)S(1)}, bf16[32,32,128]{2,1,0:T(8,128)(2,1)}, u32[]{:S(2)}) copy-start(bf16[32,32,128]{2,1,0:T(8,128)(2,1)} %copy-done.6) | copy-start | bytes 786436
  488.1 8.2 %copy-start.17 = (bf16[32,32,128]{2,1,0:T(8,128)(2,1)S(1)}, bf16[32,32,128]{2,1,0:T(8,128)(2,1)}, u32[]{:S(2)}) copy-start(bf16[32,32,128]{2,1,0:T(8,128)(2,1)} %copy-done.16) | copy-start | bytes 786436
  488.1 8.5 %copy-start.19 = (bf16[33,32,128]{2,1,0:T(8,128)(2,1)S(1)}, bf16[33,32,128]{2,1,0:T(8,128)(2,1)}, u32[]{:S(2)}) copy-start(bf16[33,32,128]{2,1,0:T(8,128)(2,1)} %copy-done.18) | copy-start | bytes 811012
  488.1 16.7 %copy-start.5 = (bf16[3,3,128,128]{3,2,1,0:T(8,128)(2,1)S(1)}, bf16[3,3,128,128]{3,2,1,0:T(8,128)(2,1)}, u32[]{:S(2)}) copy-start(bf16[3,3,128,128]{3,2,1,0:T(8,128)(2,1)} %param.11) | copy-start | bytes 884740
  488.6 9.4 %collective-permute-start.5 = (bf16[1,32,128]{2,1,0:T(8,128)(2,1)S(1)}, bf16[1,32,128]{2,1,0:T(8,128)(2,1)S(1)}, u32[]{:S(2)}, u32[]{:S(2)}) collective-permute-start(bf16[1,32,128]{2,1,0:T(8,128)(2,1)S(1)} %get-tuple-element.27), channel_id=1, source_target_pairs={{8,0},{16,8},{24,16},{32,24},{40,32},{48,40},{56,48},{64,56},{72,6... | collective-permute-start | bytes 24584 | tf_op jit(solution)/shard_map/ppermute | solution.py:22
  489.9 8.1 %collective-permute-start.4 = (bf16[1,32,128]{2,1,0:T(8,128)(2,1)S(1)}, bf16[1,32,128]{2,1,0:T(8,128)(2,1)S(1)}, u32[]{:S(2)}, u32[]{:S(2)}) collective-permute-start(bf16[1,32,128]{2,1,0:T(8,128)(2,1)S(1)} %get-tuple-element.26), channel_id=1, source_target_pairs={{0,8},{8,16},{16,24},{24,32},{32,40},{40,48},{48,56},{56,64},{64,7... | collective-permute-start | bytes 24584 | tf_op jit(solution)/shard_map/ppermute | solution.py:20
  497.2 0.8 copy-start.20
  498.1 7.0 %collective-permute-start.6 = (bf16[34,1,128]{2,1,0:T(2,128)(2,1)S(1)}, bf16[34,1,128]{2,1,0:T(2,128)(2,1)S(1)}, u32[]{:S(2)}, u32[]{:S(2)}) collective-permute-start(bf16[34,1,128]{2,1,0:T(2,128)(2,1)S(1)} %get-tuple-element.17), channel_id=1, source_target_pairs={{1,0},{2,1},{3,2},{4,3},{5,4},{6,5},{7,6},{9,8},{10,9},{11,10},{12... | collective-permute-start | bytes 26120 | tf_op jit(solution)/shard_map/ppermute | solution.py:22
  501.4 4.3 collective-permute-start.7
  506.1 139.5 %copy-start.1 = (bf16[1,512,3]{1,2,0:T(4,128)(2,1)S(1)}, bf16[1,512,3]{1,2,0:T(4,128)(2,1)}, u32[]{:S(2)}) copy-start(bf16[1,512,3]{1,2,0:T(4,128)(2,1)} %param.18) | copy-start | bytes 9220
Sparse Core Ops, SparseCore 0:
  498.1 145.4 all-reduce.2
where the time goes:
time: 655 us; the launch traced here: 652 us
  waiting for transfers between devices  282 us (43%)
  local copies, waits for them, and re-layouts  199 us (30%)
  other arithmetic  73.1 us (11%)
  starting transfers between devices  52.3 us (8%)
  matrix products  31.7 us (5%)
  between operations  15 us (2%)
    psum x1, waiting for transfers between devices, local(): grad_conv = lax.psum(local_taps, ('ra', 'dec'))  135 us
    gather x1, local copies, waits for them, and re-layouts, local(): activation[row_index, col_index].reshape(object_count, crop_size)  108 us
    all_to_all x1, waiting for transfers between devices, local(): lax.all_to_all(send_rows.reshape(owners_all, capacity, crop_size), ('ra',...  76 us
    all_to_all x1, waiting for transfers between devices, local(): lax.all_to_all(crop_grad.reshape(owners_all, capacity, crop_size), ('ra',...  67.3 us
    unnamed x4, other arithmetic  56.2 us
    gather x2, local copies, waits for them, and re-layouts, local(): jnp.take(crop_rows, slot_safe, axis=0)  17.2 us
    ppermute x4, starting transfers between devices, padded_2(): lax.ppermute(tail, axis, [(i, (i + 1) % count) for i in range(ends)])  15.1 us
    gather x2, local copies, waits for them, and re-layouts, local(): back_rows = jnp.take(returned.reshape(-1, crop_size), slot_index, axis=0)  14.1 us
  transfers between devices with their start and end apart: 12, of which 6 were waited for; matrix products, arithmetic and copies ran while one was open for 25% of the time, Pallas kernels for 0%

commit v1 on v0

--- a/solution.py
+++ b/solution.py
@@ -59,12 +59,21 @@
     return (grad_one.astype(jnp.bfloat16), crop_grad.astype(jnp.bfloat16))
 
 
+def all_sum(partial, axes, parts):
+    flat = partial.reshape(parts, -1)
+    gathered = lax.all_to_all(flat, axes, 0, 0, tiled=True)
+    chunk = jnp.sum(gathered, axis=0, keepdims=True)
+    spread = lax.all_to_all(jnp.broadcast_to(chunk, flat.shape), axes, 0, 0, tiled=True)
+    return spread.reshape(partial.shape)
+
+
 def local(
     features, conv_weight, conv_bias, corners, owner_ids, labels, head_w1, head_b1, head_w2, head_b2
 ):
     tile_rows, tile_cols, channels = features.shape
+    cells_all = tile_rows * tile_cols
     padded = padded_2(features, (("ra", 0), ("dec", 1)), 1)
-    pre_conv = jnp.zeros((tile_rows * tile_cols, channels), jnp.float32)
+    pre_conv = jnp.zeros((cells_all, channels), jnp.float32)
     for row_off in range(3):
         for col_off in range(3):
             window = padded[row_off : row_off + tile_rows, col_off : col_off + tile_cols].reshape(
@@ -73,7 +82,7 @@
             pre_conv = pre_conv + jnp.dot(
                 window, conv_weight[row_off, col_off], preferred_element_type=jnp.float32
             )
-    pre_conv = (pre_conv + conv_bias[None, :]).reshape(tile_rows, tile_cols, channels)
+    pre_conv = pre_conv + conv_bias[None, :]
     activation = jax.nn.silu(pre_conv).astype(jnp.bfloat16)
     count_ra = lax.axis_size("ra")
     count_dec = lax.axis_size("dec")
@@ -84,16 +93,10 @@
     capacity = (object_count + owners_all - 1) // owners_all + 1
     slot_total = owners_all * capacity
     classes = head_w2.shape[2]
-    crop_size = CROP * CROP * channels
+    cells_crop = CROP * CROP
+    crop_size = cells_crop * channels
     slot_rank = rank_in_owner(owner_list, owners_all)
     slot_index = owner_list * capacity + slot_rank
-    offsets = jnp.arange(CROP, dtype=jnp.int32)
-    row_index = corner_list[:, 0][:, None, None] + offsets[None, :, None]
-    col_index = corner_list[:, 1][:, None, None] + offsets[None, None, :]
-    crop_rows = activation[row_index, col_index].reshape(object_count, crop_size)
-    onehot_label = (
-        labels.reshape(-1)[:, None] == jnp.arange(classes, dtype=jnp.int32)[None, :]
-    ).astype(jnp.bfloat16)
     slot_object = (
         jnp.full((slot_total,), -1, jnp.int32)
         .at[slot_index]
@@ -101,59 +104,48 @@
     )
     slot_live = slot_object >= 0
     slot_safe = jnp.where(slot_live, slot_object, 0)
-    send_rows = jnp.where(
-        slot_live[:, None], jnp.take(crop_rows, slot_safe, axis=0), jnp.zeros((), jnp.bfloat16)
+    slot_row = jnp.take(corner_list[:, 0], slot_safe)
+    slot_col = jnp.take(corner_list[:, 1], slot_safe)
+    cell_step = jnp.arange(cells_crop, dtype=jnp.int32)
+    cell_at = (slot_row[:, None] + cell_step[None, :] // CROP) * tile_cols + (
+        slot_col[:, None] + cell_step[None, :] % CROP
     )
-    send_target = jnp.where(
-        slot_live[:, None], jnp.take(onehot_label, slot_safe, axis=0), jnp.zeros((), jnp.bfloat16)
-    )
-    weight_one = head_w1[0]
-    bias_one = head_b1[0]
-    weight_two = head_w2[0]
-    bias_two = head_b2[0]
-    got_rows, got_target = (
-        lax.all_to_all(
-            send_rows.reshape(owners_all, capacity, crop_size),
-            ("ra", "dec"),
-            split_axis=0,
-            concat_axis=0,
-            tiled=True,
-        ),
-        lax.all_to_all(
-            send_target.reshape(owners_all, capacity, classes),
-            ("ra", "dec"),
-            split_axis=0,
-            concat_axis=0,
-            tiled=True,
-        ),
-    )
+    cell_at = jnp.where(slot_live[:, None], cell_at, -1).reshape(owners_all, capacity * cells_crop)
+    picker = (
+        cell_at[:, :, None] == jnp.arange(cells_all, dtype=jnp.int32)[None, None, :]
+    ).astype(jnp.bfloat16)
+    crops = jnp.einsum(
+        "dny,yf->dnf", picker, activation, preferred_element_type=jnp.float32
+    ).astype(jnp.bfloat16)
+    slot_label = jnp.take(labels.reshape(-1), slot_safe)
+    label_code = jnp.where(
+        slot_live, (jnp.arange(slot_total, dtype=jnp.int32) % capacity) * classes + slot_label, -1
+    ).reshape(owners_all, capacity)
+    label_row = jnp.any(
+        label_code[:, :, None] == jnp.arange(channels, dtype=jnp.int32)[None, None, :], axis=1
+    ).astype(jnp.bfloat16)
+    send = jnp.concatenate([crops, label_row[:, None, :]], axis=1)
+    got = lax.all_to_all(send, ("ra", "dec"), split_axis=0, concat_axis=0, tiled=True)
+    got_rows = got[:, : capacity * cells_crop, :].reshape(slot_total, crop_size)
+    got_target = got[:, capacity * cells_crop, : capacity * classes].reshape(slot_total, classes)
     grad_one, crop_grad = head_pass(
-        got_rows.reshape(-1, crop_size),
-        got_target.reshape(-1, classes),
-        weight_one,
-        bias_one,
-        weight_two,
-        bias_two,
+        got_rows, got_target, head_w1[0], head_b1[0], head_w2[0], head_b2[0]
     )
     returned = lax.all_to_all(
-        crop_grad.reshape(owners_all, capacity, crop_size),
+        crop_grad.reshape(owners_all, capacity * cells_crop, channels),
         ("ra", "dec"),
         split_axis=0,
         concat_axis=0,
         tiled=True,
     )
-    back_rows = jnp.take(returned.reshape(-1, crop_size), slot_index, axis=0)
-    values = back_rows.reshape(object_count, CROP, CROP, channels).astype(jnp.float32)
-    act_grad = (
-        jnp.zeros((tile_rows, tile_cols, channels), jnp.float32)
-        .at[row_index, col_index]
-        .add(values)
+    act_grad = jnp.einsum("dny,dnf->yf", picker, returned, preferred_element_type=jnp.float32)
+    pre_grad = (act_grad * silu_slope(pre_conv)).astype(jnp.bfloat16).reshape(
+        tile_rows, tile_cols, channels
     )
-    pre_grad = (act_grad * silu_slope(pre_conv)).astype(jnp.bfloat16)
     grad_padded = padded_2(pre_grad, (("ra", 0), ("dec", 1)), 1)
     pre_flat = pre_grad.reshape(-1, channels)
     tap_list = []
-    grad_feat = jnp.zeros((tile_rows * tile_cols, channels), jnp.float32)
+    grad_feat = jnp.zeros((cells_all, channels), jnp.float32)
     for row_off in range(3):
         for col_off in range(3):
             window = padded[row_off : row_off + tile_rows, col_off : col_off + tile_cols].reshape(
@@ -174,7 +166,7 @@
                 preferred_element_type=jnp.float32,
             )
     local_taps = jnp.stack(tap_list).reshape(3, 3, channels, channels)
-    grad_conv = lax.psum(local_taps, ("ra", "dec"))
+    grad_conv = all_sum(local_taps, ("ra", "dec"), owners_all)
     grad_features = grad_feat.reshape(tile_rows, tile_cols, channels).astype(jnp.bfloat16)
     return (grad_features, grad_conv, grad_one[None])
 

time: 655 us -> 313 us (0.48)
  waiting for transfers between devices: 282 us -> 74.6 us
  local copies, waits for them, and re-layouts: 199 us -> 39.6 us
  blocking collectives: 0 us -> 72.4 us
  other arithmetic: 73.1 us -> 4.8 us
  matrix products: 31.7 us -> 76 us
  between operations: 15 us -> 1.57 us
  starting transfers between devices: 52.3 us -> 39.5 us
    psum x1 -> x0, waiting for transfers between devices: 135 us -> none  [local(): grad_conv = lax.psum(local_taps, ('ra', 'dec'))]
    gather x8 -> x3, local copies, waits for them, and re-layouts: 141 us -> 8.45 us  [the longest x1 2.82 us: local(): slot_col = jnp.take(corner_list[:, 1], slot_safe)]
    all_to_all x3, waiting for transfers between devices: 143 us -> 69.6 us  [the longest x1 52.2 us: local(): lax.all_to_all(crop_grad.reshape(owners_all, capacity * cells_crop, chann...]
    all_to_all x0 -> x1, blocking collectives: none -> 72.4 us  [local(): lax.all_to_all(send, ('ra', 'dec'), split_axis=0, concat_axis=0, tiled=True)]
    unnamed x4 -> x0, other arithmetic: 56.2 us -> none
    dot_general x0 -> x2, matrix products: none -> 35.8 us  [the longest x1 21.1 us: local(): jnp.einsum('dny,yf->dnf', picker, activation, preferred_element_type=jnp....]
    reshape x4 -> x2, local copies, waits for them, and re-layouts: 40.9 us -> 19.1 us  [the longest x1 9.8 us: local(): crop_grad.reshape(owners_all, capacity * cells_crop, channels)]
    all_to_all x3, starting transfers between devices: 29.1 us -> 17.2 us  [the longest x1 6.75 us: all_sum(): gathered = lax.all_to_all(flat, axes, 0, 0, tiled=True)]
  transfers between devices with their start and end apart: 12 -> 11, of which waited for: 6 -> 5; matrix products, arithmetic and copies ran while one was open for 25% -> 11% of each run, Pallas kernels for 0% -> 0%
where the time goes in v1:
time: 313 us; the launch traced here: 308 us
  matrix products  76 us (24%)
  waiting for transfers between devices  74.6 us (24%)
  blocking collectives  72.4 us (23%)
  local copies, waits for them, and re-layouts  39.6 us (13%)
  starting transfers between devices  39.5 us (13%)
  other arithmetic  4.8 us (2%)
    all_to_all x1, blocking collectives, local(): lax.all_to_all(send, ('ra', 'dec'), split_axis=0, concat_axis=0, tiled=True)  72.4 us
    all_to_all x1, waiting for transfers between devices, local(): lax.all_to_all(crop_grad.reshape(owners_all, capacity * cells_crop, chann...  52.2 us
    dot_general x1, matrix products, local(): jnp.einsum('dny,yf->dnf', picker, activation, preferred_element_type=jnp....  21.1 us
    ppermute x4, starting transfers between devices, padded_2(): lax.ppermute(tail, axis, [(i, (i + 1) % count) for i in range(ends)])  14.8 us
    dot_general x1, matrix products, local(): jnp.einsum('dny,dnf->yf', picker, returned, preferred_element_type=jnp.fl...  14.7 us
    all_to_all x1, waiting for transfers between devices, all_sum(): lax.all_to_all(jnp.broadcast_to(chunk, flat.shape), axes, 0, 0, tiled=True)  13 us
    reshape x1, local copies, waits for them, and re-layouts, local(): crop_grad.reshape(owners_all, capacity * cells_crop, channels)  9.8 us
    reshape x1, local copies, waits for them, and re-layouts, local(): got_rows = got[:, :capacity * cells_crop, :].reshape(slot_total, crop_size)  9.35 us
  transfers between devices with their start and end apart: 11, of which 5 were waited for; matrix products, arithmetic and copies ran while one was open for 11% of the time, Pallas kernels for 0%

profile of v1, /device:TPU:1, one launch (start us, length us, event | category | flops | bytes accessed | tf_op | source)
XLA Modules:
  0.0 308.4 jit_solution(16895672889194569484)
XLA Ops:
  0.7 0.8 fusion.127
  1.4 4.0 %collective-permute-start = (bf16[1,32,128]{2,1,0:T(8,128)(2,1)S(1)}, bf16[1,32,128]{2,1,0:T(8,128)(2,1)S(1)}, u32[]{:S(2)}, u32[]{:S(2)}) collective-permute-start(bf16[1,32,128]{2,1,0:T(8,128)(2,1)S(1)} %get-tuple-element.37), channel_id=1, source_target_pairs={{0,8},{8,16},{16,24},{24,32},{32,40},{40,48},{48,56},{56,64},{64,7... | collective-permute-start | bytes 24584 | tf_op jit(solution)/shard_map/ppermute | solution.py:20
  5.5 1.3 collective-permute-start.1
  6.8 0.8 fusion.128
  7.6 0.8 iota_compare_fusion.12
  8.6 0.9 fusion.63
  9.5 0.7 compare_select_fusion
  10.2 1.2 scatter_custom_fusion
  11.4 2.8 gather_fusion
  14.2 2.8 gather_fusion.1
  17.1 2.8 gather_fusion.2
  19.9 0.2 broadcast_in_dim.50
  21.9 4.0 %collective-permute-start.2 = (bf16[34,1,128]{2,1,0:T(2,128)(2,1)S(1)}, bf16[34,1,128]{2,1,0:T(2,128)(2,1)S(1)}, u32[]{:S(2)}, u32[]{:S(2)}) collective-permute-start(bf16[34,1,128]{2,1,0:T(2,128)(2,1)S(1)} %get-tuple-element.27), channel_id=1, source_target_pairs={{0,1},{1,2},{2,3},{3,4},{4,5},{5,6},{6,7},{8,9},{9,10},{10,11},{11... | collective-permute-start | bytes 26120 | tf_op jit(solution)/shard_map/ppermute | solution.py:20
  25.9 1.9 collective-permute-start.3
  28.3 2.7 collective-permute-done.3
  30.9 0.4 pad_maximum_fusion.6
  32.0 0.2 convolution_add_fusion.10
  32.2 0.2 convolution_add_fusion.9
  32.6 0.2 fusion.16
  32.9 21.1 %fusion.9 = bf16[128,147,128]{2,0,1:T(8,128)(2,1)S(1)} fusion(s32[128,147]{0,1:T(8,128)S(1)} %add_select_fusion, f32[1024,128]{1,0:T(8,128)S(1)} %fusion.16), kind=kOutput, calls=%fused_computation.17 | convolution fusion | flops 4954832896 | bytes 5416448 | tf_op jit(solution)/shard_map/dny,yf->dnf/dot_general | solution.py:117
  54.0 0.4 pad_maximum_fusion
  54.4 3.1 %copy.43 = bf16[128,148,128]{2,1,0:T(8,128)(2,1)S(1)} copy(bf16[128,148,128]{2,0,1:T(8,128)(2,1)S(1)} %pad_maximum_fusion) | data formatting | bytes 9699328 | tf_op jit(solution)/shard_map/concatenate | solution.py:127
  57.6 72.4 %all_to_all.25 = bf16[128,148,128]{2,1,0:T(8,128)(2,1)S(1)} all-to-all(bf16[128,148,128]{2,1,0:T(8,128)(2,1)S(1)} %copy.43), channel_id=1, replica_groups=mesh['ra'=16,'dec'=8] {'ra','dec'}, dimensions={0} | all-to-all | bytes 9699328 | tf_op jit(solution)/shard_map/all_to_all | solution.py:128
  129.9 2.3 copy-done.3
  132.2 0.2 fusion.64
  132.6 9.3 %reshape.271 = bf16[384,6272]{1,0:T(8,128)(2,1)} reshape(bf16[128,147,128]{2,1,0:T(8,128)(2,1)} %bitcast.207) | data formatting | bytes 9633792 | tf_op jit(solution)/shard_map/reshape | solution.py:129
  142.1 7.9 %fusion.10 = f32[384,512]{1,0:T(8,128)} fusion(bf16[384,6272]{1,0:T(8,128)(2,1)} %reshape.271, bf16[1,6272,512]{2,1,0:T(8,128)(2,1)} %param.18, f32[512]{0:T(512)S(1)} %bitcast.246), kind=kOutput, calls=%fused_computation.19 | convolution fusion | flops 2466447360 | bytes 12027904 | tf_op jit(solution)/shard_map/dot_general | solution.py:43
  150.0 2.9 fusion.13
  153.0 7.9 %convolution_convert_fusion.1 = bf16[384,6272]{1,0:T(8,128)(2,1)} fusion(bf16[384,512]{1,0:T(8,128)(2,1)} %fusion.13, bf16[1,6272,512]{2,1,0:T(8,128)(2,1)} %param.18), kind=kOutput, calls=%fused_computation.10 | convolution fusion | flops 2468659200 | bytes 11632640 | tf_op jit(solution)/shard_map/dot_general | solution.py:56
  160.9 9.8 %reshape.272 = bf16[128,147,128]{2,1,0:T(8,128)(2,1)} reshape(bf16[384,6272]{1,0:T(8,128)(2,1)} %convolution_convert_fusion.1) | data formatting | bytes 9633792 | tf_op jit(solution)/shard_map/reshape | solution.py:135
  170.7 5.7 %all-to-all-start.1 = ((bf16[128,147,128]{2,1,0:T(8,128)(2,1)}), bf16[128,147,128]{2,1,0:T(8,128)(2,1)}, u32[]{:S(2)}, u32[]{:S(2)}) async-start(bf16[128,147,128]{2,1,0:T(8,128)(2,1)} %reshape.272), calls=%async_computation.1 | async-start | bytes 9961472 | tf_op jit(solution)/shard_map/all_to_all | solution.py:134
  176.4 8.7 %fusion.4 = bf16[1,6272,512]{2,1,0:T(8,128)(2,1)} fusion(bf16[384,6272]{1,0:T(8,128)(2,1)} %reshape.271, bf16[384,512]{1,0:T(8,128)(2,1)} %fusion.13), kind=kOutput, calls=%fused_computation.11 | convolution fusion | flops 2469462016 | bytes 11632640 | tf_op jit(solution)/shard_map/dot_general | solution.py:53
  185.2 52.2 %all-to-all-done.1 = bf16[128,147,128]{2,1,0:T(8,128)(2,1)} async-done(((bf16[128,147,128]{2,1,0:T(8,128)(2,1)}), bf16[128,147,128]{2,1,0:T(8,128)(2,1)}, u32[]{:S(2)}, u32[]{:S(2)}) %all-to-all-start.1) | async-done | bytes 4816928 | tf_op jit(solution)/shard_map/all_to_all | solution.py:134
  237.4 14.7 %fusion.25 = bf16[1024,128]{1,0:T(8,128)(2,1)S(1)} fusion(bf16[128,147,128]{2,1,0:T(8,128)(2,1)} %all-to-all-done.1, s32[128,147]{0,1:T(8,128)S(1)} %add_select_fusion, f32[1024,128]{1,0:T(8,128)S(1)} %fusion.16), kind=kOutput, calls=%fused_computation.41 | convolution fusion | flops 4952948736 | bytes 5678592 | tf_op jit(solution)/shard_map/dny,dnf->yf/dot_general | solution.py:141
  252.1 0.9 fusion.36
  253.0 1.3 collective-permute-start.5
  254.3 4.0 %collective-permute-start.4 = (bf16[1,32,128]{2,1,0:T(8,128)(2,1)S(1)}, bf16[1,32,128]{2,1,0:T(8,128)(2,1)S(1)}, u32[]{:S(2)}, u32[]{:S(2)}) collective-permute-start(bf16[1,32,128]{2,1,0:T(8,128)(2,1)S(1)} %get-tuple-element.31), channel_id=1, source_target_pairs={{0,8},{8,16},{16,24},{24,32},{32,40},{40,48},{48,56},{56,64},{64,7... | collective-permute-start | bytes 24584 | tf_op jit(solution)/shard_map/ppermute | solution.py:20
  258.3 0.9 fusion.35
  259.2 0.9 fusion.34
  260.1 0.9 fusion.33
  261.0 0.9 fusion.32
  261.9 0.9 fusion.31
  262.8 0.9 fusion.30
  263.7 0.9 fusion.29
  264.6 0.9 fusion.28
  265.5 6.8 %all-to-all-start.2 = ((f32[128,1,1152]{2,1,0:T(1,128)}), f32[128,1,1152]{2,1,0:T(1,128)S(1)}, u32[]{:S(2)}, u32[]{:S(2)}) async-start(f32[128,1,1152]{2,1,0:T(1,128)} %bitcast.59), calls=%async_computation.2 | async-start | bytes 1179648 | tf_op jit(solution)/shard_map/all_to_all | solution.py:64
  272.3 3.0 collective-permute-start.6
  275.3 2.8 collective-permute-start.7
  278.2 0.2 fusion.82
  278.4 2.3 collective-permute-done.6
  281.1 0.2 convolution_add_fusion.6
  281.4 0.2 convolution_add_fusion.5
  281.6 0.2 convolution_add_fusion.4
  281.9 0.2 convolution_add_fusion.3
  282.1 0.2 convolution_add_fusion.2
  282.3 4.4 %all-to-all-done.2 = f32[128,1,1152]{2,1,0:T(1,128)S(1)} async-done(((f32[128,1,1152]{2,1,0:T(1,128)}), f32[128,1,1152]{2,1,0:T(1,128)S(1)}, u32[]{:S(2)}, u32[]{:S(2)}) %all-to-all-start.2) | async-done | bytes 589856 | tf_op jit(solution)/shard_map/all_to_all | solution.py:64
  286.7 0.4 reduce_sum.29
  287.1 1.1 broadcast_in_dim.54
  288.2 4.7 %all-to-all-start.3 = ((f32[128,1,1152]{2,1,0:T(1,128)}), f32[128,1,1152]{2,1,0:T(1,128)S(1)}, u32[]{:S(2)}, u32[]{:S(2)}) async-start(f32[128,1,1152]{2,1,0:T(1,128)} %broadcast_in_dim.54), calls=%async_computation.3 | async-start | bytes 1179648 | tf_op jit(solution)/shard_map/all_to_all | solution.py:66
  292.9 0.2 fusion.65
  293.1 0.2 convolution_add_fusion.1
  293.3 0.9 fusion.24
  294.3 13.0 %all-to-all-done.3 = f32[128,1,1152]{2,1,0:T(1,128)S(1)} async-done(((f32[128,1,1152]{2,1,0:T(1,128)}), f32[128,1,1152]{2,1,0:T(1,128)S(1)}, u32[]{:S(2)}, u32[]{:S(2)}) %all-to-all-start.3) | async-done | bytes 589856 | tf_op jit(solution)/shard_map/all_to_all | solution.py:66
  307.3 0.8 copy.71
  (77 shorter events, 4.0 us)
Async XLA Ops:
  0.6 149.4 %copy-start = (bf16[1,512,3]{1,2,0:T(4,128)(2,1)S(1)}, bf16[1,512,3]{1,2,0:T(4,128)(2,1)}, u32[]{:S(2)}) copy-start(bf16[1,512,3]{1,2,0:T(4,128)(2,1)} %param.20) | copy-start | bytes 9220
  0.6 21.0 %copy-start.4 = (bf16[32,32,128]{2,1,0:T(8,128)(2,1)S(1)}, bf16[32,32,128]{2,1,0:T(8,128)(2,1)}, u32[]{:S(2)}) copy-start(bf16[32,32,128]{2,1,0:T(8,128)(2,1)} %param.12) | copy-start | bytes 786436
  0.7 16.4 %copy-start.2 = (s32[1,1,200]{2,1,0:T(1,128)S(1)}, s32[1,1,200]{2,1,0:T(1,128)}, u32[]{:S(2)}) copy-start(s32[1,1,200]{2,1,0:T(1,128)} %param.17) | copy-start | bytes 2404
  1.4 20.2 %collective-permute-start = (bf16[1,32,128]{2,1,0:T(8,128)(2,1)S(1)}, bf16[1,32,128]{2,1,0:T(8,128)(2,1)S(1)}, u32[]{:S(2)}, u32[]{:S(2)}) collective-permute-start(bf16[1,32,128]{2,1,0:T(8,128)(2,1)S(1)} %get-tuple-element.37), channel_id=1, source_target_pairs={{0,8},{8,16},{16,24},{24,32},{32,40},{40,48},{48,56},{56,64},{64,7... | collective-permute-start | bytes 24584 | tf_op jit(solution)/shard_map/ppermute | solution.py:20
  5.5 16.2 %collective-permute-start.1 = (bf16[1,32,128]{2,1,0:T(8,128)(2,1)S(1)}, bf16[1,32,128]{2,1,0:T(8,128)(2,1)S(1)}, u32[]{:S(2)}, u32[]{:S(2)}) collective-permute-start(bf16[1,32,128]{2,1,0:T(8,128)(2,1)S(1)} %get-tuple-element.36), channel_id=1, source_target_pairs={{8,0},{16,8},{24,16},{32,24},{40,32},{48,40},{56,48},{64,56},{72,6... | collective-permute-start | bytes 24584 | tf_op jit(solution)/shard_map/ppermute | solution.py:22
  8.3 19.5 %copy-start.5 = (bf16[3,3,128,128]{3,2,1,0:T(8,128)(2,1)S(1)}, bf16[3,3,128,128]{3,2,1,0:T(8,128)(2,1)}, u32[]{:S(2)}) copy-start(bf16[3,3,128,128]{3,2,1,0:T(8,128)(2,1)} %param.13) | copy-start | bytes 884740
  21.9 6.3 %collective-permute-start.2 = (bf16[34,1,128]{2,1,0:T(2,128)(2,1)S(1)}, bf16[34,1,128]{2,1,0:T(2,128)(2,1)S(1)}, u32[]{:S(2)}, u32[]{:S(2)}) collective-permute-start(bf16[34,1,128]{2,1,0:T(2,128)(2,1)S(1)} %get-tuple-element.27), channel_id=1, source_target_pairs={{0,1},{1,2},{2,3},{3,4},{4,5},{5,6},{6,7},{8,9},{9,10},{10,11},{11... | collective-permute-start | bytes 26120 | tf_op jit(solution)/shard_map/ppermute | solution.py:20
  25.9 5.1 %collective-permute-start.3 = (bf16[34,1,128]{2,1,0:T(2,128)(2,1)S(1)}, bf16[34,1,128]{2,1,0:T(2,128)(2,1)S(1)}, u32[]{:S(2)}, u32[]{:S(2)}) collective-permute-start(bf16[34,1,128]{2,1,0:T(2,128)(2,1)S(1)} %get-tuple-element.28), channel_id=1, source_target_pairs={{1,0},{2,1},{3,2},{4,3},{5,4},{6,5},{7,6},{9,8},{10,9},{11,10},{12... | collective-permute-start | bytes 26120 | tf_op jit(solution)/shard_map/ppermute | solution.py:22
  28.0 4.6 %copy-start.6 = (f32[128]{0:T(128)S(1)}, f32[128]{0:T(128)}, u32[]{:S(2)}) copy-start(f32[128]{0:T(128)} %param.14) | copy-start | bytes 1540
  129.9 2.3 copy-start.3
  132.6 9.5 %copy-start.7 = (f32[1,512]{1,0:T(1,128)S(1)}, f32[1,512]{1,0:T(1,128)}, u32[]{:S(2)}) copy-start(f32[1,512]{1,0:T(1,128)} %param.19) | copy-start | bytes 6148
  142.1 7.9 %copy-start.8 = (f32[1,3]{1,0:T(1,128)S(1)}, f32[1,3]{1,0:T(1,128)}, u32[]{:S(2)}) copy-start(f32[1,3]{1,0:T(1,128)} %param.21) | copy-start | bytes 40
  170.7 66.7 %all-to-all-start.1 = ((bf16[128,147,128]{2,1,0:T(8,128)(2,1)}), bf16[128,147,128]{2,1,0:T(8,128)(2,1)}, u32[]{:S(2)}, u32[]{:S(2)}) async-start(bf16[128,147,128]{2,1,0:T(8,128)(2,1)} %reshape.272), calls=%async_computation.1 | async-start | bytes 9961472 | tf_op jit(solution)/shard_map/all_to_all | solution.py:134
  253.0 19.3 %collective-permute-start.5 = (bf16[1,32,128]{2,1,0:T(8,128)(2,1)S(1)}, bf16[1,32,128]{2,1,0:T(8,128)(2,1)S(1)}, u32[]{:S(2)}, u32[]{:S(2)}) collective-permute-start(bf16[1,32,128]{2,1,0:T(8,128)(2,1)S(1)} %get-tuple-element.32), channel_id=1, source_target_pairs={{8,0},{16,8},{24,16},{32,24},{40,32},{48,40},{56,48},{64,56},{72,6... | collective-permute-start | bytes 24584 | tf_op jit(solution)/shard_map/ppermute | solution.py:22
  254.3 18.0 %collective-permute-start.4 = (bf16[1,32,128]{2,1,0:T(8,128)(2,1)S(1)}, bf16[1,32,128]{2,1,0:T(8,128)(2,1)S(1)}, u32[]{:S(2)}, u32[]{:S(2)}) collective-permute-start(bf16[1,32,128]{2,1,0:T(8,128)(2,1)S(1)} %get-tuple-element.31), channel_id=1, source_target_pairs={{0,8},{8,16},{16,24},{24,32},{32,40},{40,48},{48,56},{56,64},{64,7... | collective-permute-start | bytes 24584 | tf_op jit(solution)/shard_map/ppermute | solution.py:20
  265.5 21.2 %all-to-all-start.2 = ((f32[128,1,1152]{2,1,0:T(1,128)}), f32[128,1,1152]{2,1,0:T(1,128)S(1)}, u32[]{:S(2)}, u32[]{:S(2)}) async-start(f32[128,1,1152]{2,1,0:T(1,128)} %bitcast.59), calls=%async_computation.2 | async-start | bytes 1179648 | tf_op jit(solution)/shard_map/all_to_all | solution.py:64
  272.3 8.4 %collective-permute-start.6 = (bf16[34,1,128]{2,1,0:T(2,128)(2,1)S(1)}, bf16[34,1,128]{2,1,0:T(2,128)(2,1)S(1)}, u32[]{:S(2)}, u32[]{:S(2)}) collective-permute-start(bf16[34,1,128]{2,1,0:T(2,128)(2,1)S(1)} %get-tuple-element.22), channel_id=1, source_target_pairs={{1,0},{2,1},{3,2},{4,3},{5,4},{6,5},{7,6},{9,8},{10,9},{11,10},{12... | collective-permute-start | bytes 26120 | tf_op jit(solution)/shard_map/ppermute | solution.py:22
  275.3 5.4 %collective-permute-start.7 = (bf16[34,1,128]{2,1,0:T(2,128)(2,1)S(1)}, bf16[34,1,128]{2,1,0:T(2,128)(2,1)S(1)}, u32[]{:S(2)}, u32[]{:S(2)}) collective-permute-start(bf16[34,1,128]{2,1,0:T(2,128)(2,1)S(1)} %get-tuple-element.23), channel_id=1, source_target_pairs={{0,1},{1,2},{2,3},{3,4},{4,5},{5,6},{6,7},{8,9},{9,10},{10,11},{11... | collective-permute-start | bytes 26120 | tf_op jit(solution)/shard_map/ppermute | solution.py:20
  281.6 26.5 %copy-start.1 = (bf16[1,512,3]{1,2,0:T(4,128)(2,1)S(1)}, bf16[1,512,3]{1,2,0:T(4,128)(2,1)}, u32[]{:S(2)}) copy-start(bf16[1,512,3]{1,2,0:T(4,128)(2,1)} %param.20) | copy-start | bytes 9220
  288.2 19.1 %all-to-all-start.3 = ((f32[128,1,1152]{2,1,0:T(1,128)}), f32[128,1,1152]{2,1,0:T(1,128)S(1)}, u32[]{:S(2)}, u32[]{:S(2)}) async-start(f32[128,1,1152]{2,1,0:T(1,128)} %broadcast_in_dim.54), calls=%async_computation.3 | async-start | bytes 1179648 | tf_op jit(solution)/shard_map/all_to_all | solution.py:66
